TPU v7x, 32 devices: a whole 2x2x4 slice. The times are simulated.
32 devices in a mesh: group: 4 (over y, core), gx: 4 (over z), gy: 2 (over x).
Axes of the slice: x: 2, y: 2, z: 4, core: 2. Of those that a mesh axis runs over, the one named last changes fastest.
Arguments:
- populations: bfloat16 [19, 32, 16, 128], P(None, ('group', 'gx'), 'gy'), may hold values from 0 to 1, as said below
- solid_mask: int32 [32, 16, 128], P(('group', 'gx'), 'gy'), may hold values 0 or 1
- wall_cells: int32 [16, 2, 512], P(('group', 'gx'), 'gy'), may hold values from 0 to 2047
- body_load: float32 [3, 64, 8, 128], P(None, ('group', 'gx'), 'gy'), may hold values from -3 to 3
- elem_scale: float32 [64, 8, 128], P(('group', 'gx'), 'gy'), may hold values from 0.05 to 0.5
- elem_active: int32 [64, 8, 128], P(('group', 'gx'), 'gy'), may hold values 0 or 1
- elem_matrix: float32 [24, 24], replicated, may hold values from -0.25 to 8, as said below
- iface_nodes: int32 [16, 2, 256], P(('group', 'gx'), 'gy'), may hold values from 0 to 2047
- iface_coords: float32 [3, 16, 2, 256], P(None, ('group', 'gx'), 'gy'), may hold values from 0 to 128
- neighbours: int32 [16, 2, 2, 8], P(('group', 'gx'), 'gy'), may hold values from 0 to 11, as said below
Outputs:
- new_populations: bfloat16 [19, 32, 16, 128], P(None, ('group', 'gx'), 'gy')
- displacement: float32 [3, 64, 8, 128], P(None, ('group', 'gx'), 'gy')
Inputs may be any that keep to these rules, and one draw needn't show every extreme that they name: `populations`: each population is positive, between 0.48 and 1.68 times its lattice weight. `elem_matrix`: symmetric. `neighbours`: on devices of structure group 3 + j every entry is g * 4 + t with t < 4, g < 3 and g congruent to j modulo 1.
All inputs are finite; a program needn't handle non-finite values. No bound on the sum of `solid_mask` or of `elem_active` on one device may be relied on, other than what follows from the above.
Results may differ from a plain program's by a relative error of at most 0.0019.
Values may be sent and summed in bfloat16 or wider, within the bound.
No kernel may reach another device: no remote copies, remote signals or barrier semaphores. Data moves between devices by JAX's collectives and lax.ppermute only.
A program may use at most 64 MiB of HBM per device.

v0:
```python
import jax
import jax.numpy as jnp
from jax import lax
from jax.sharding import PartitionSpec as P

TILE = 128
ITERS = 3
velocity = [
    (0, 0, 0),
    (1, 0, 0),
    (-1, 0, 0),
    (0, 1, 0),
    (0, -1, 0),
    (0, 0, 1),
    (0, 0, -1),
    (1, 1, 0),
    (-1, -1, 0),
    (1, -1, 0),
    (-1, 1, 0),
    (1, 0, 1),
    (-1, 0, -1),
    (1, 0, -1),
    (-1, 0, 1),
    (0, 1, 1),
    (0, -1, -1),
    (0, 1, -1),
    (0, -1, 1),
]
opposite = [0, 2, 1, 4, 3, 6, 5, 8, 7, 10, 9, 12, 11, 14, 13, 16, 15, 18, 17]
lattice_weight = [1.0 / 3.0] + [1.0 / 18.0] * 6 + [1.0 / 36.0] * 12
relax_rate = 1.0 / 0.6
wall_gain = 60.0
basis_radius = 24.0
mass_shift = 0.5


def padded(cells, sides, width):
    for axis, dim in sides:
        count = lax.axis_size(axis)
        ends = count - 1
        head = lax.slice_in_dim(cells, 0, width, axis=dim)
        tail = lax.slice_in_dim(cells, cells.shape[dim] - width, cells.shape[dim], axis=dim)
        cells = jnp.concatenate(
            [
                lax.ppermute(tail, axis, [(i, (i + 1) % count) for i in range(ends)]),
                cells,
                lax.ppermute(head, axis, [((i + 1) % count, i) for i in range(ends)]),
            ],
            axis=dim,
        )
    return cells


def passed_along(value, axis, steps):
    count = lax.axis_size(axis)
    pairs = [(source, (source + steps) % count) for source in range(count)]
    return lax.ppermute(value, axis, pairs)


def project_onto(vectors, direction):
    summed = jnp.zeros_like(vectors[0])
    for component in range(3):
        if direction[component] != 0:
            summed = summed + float(direction[component]) * vectors[component]
    return summed


def collide(population):
    density = jnp.sum(population, axis=0)
    momentum = [jnp.zeros_like(density) for component in range(3)]
    for q in range(19):
        for component in range(3):
            if velocity[q][component] != 0:
                momentum[component] = (
                    momentum[component] + float(velocity[q][component]) * population[q]
                )
    velocity_parts = [entry / density for entry in momentum]
    speed_square = (
        velocity_parts[0] * velocity_parts[0]
        + velocity_parts[1] * velocity_parts[1]
        + velocity_parts[2] * velocity_parts[2]
    )
    relaxed = []
    for q in range(19):
        project = project_onto(velocity_parts, velocity[q])
        balance = (
            lattice_weight[q]
            * density
            * (1.0 + 3.0 * project + 4.5 * project * project - 1.5 * speed_square)
        )
        relaxed.append(population[q] + relax_rate * (balance - population[q]))
    return jnp.stack(relaxed)


def stream_links(moved, fluid_ext):
    span_cells = moved.shape[1] - 2
    across_cells = moved.shape[2] - 2
    deep_cells = moved.shape[3] - 2
    upstream, opened, bounce, reflected = ([], [], [], [])
    for q in range(19):
        shift_x, shift_y, shift_z = velocity[q]
        window = (
            slice(1 - shift_x, 1 - shift_x + span_cells),
            slice(1 - shift_y, 1 - shift_y + across_cells),
            slice(1 - shift_z, 1 - shift_z + deep_cells),
        )
        upstream.append(moved[q][window])
        open_up = fluid_ext[window]
        opened.append(open_up)
        bounce.append(1.0 - open_up)
        reflected.append(
            moved[opposite[q], 1 : span_cells + 1, 1 : across_cells + 1, 1 : deep_cells + 1]
        )
    return (upstream, opened, bounce, reflected)


def wall_force(bounce, reflected):
    force_parts = [jnp.zeros_like(reflected[0]) for component in range(3)]
    for q in range(19):
        for component in range(3):
            if velocity[q][component] != 0:
                force_parts[component] = (
                    force_parts[component]
                    - 2.0 * float(velocity[q][component]) * bounce[q] * reflected[q]
                )
    return jnp.stack(force_parts)


def stream_all(moved, fluid_ext, wall_speed):
    upstream, opened, bounce, reflected = stream_links(moved, fluid_ext)
    inside = fluid_ext[1:-1, 1:-1, 1:-1]
    speed_list = [wall_speed[0], wall_speed[1], wall_speed[2]]
    result = []
    for q in range(19):
        correction = 6.0 * lattice_weight[q] * project_onto(speed_list, velocity[q])
        result.append(inside * (opened[q] * upstream[q] + bounce[q] * (reflected[q] + correction)))
    return jnp.stack(result).astype(jnp.bfloat16)


def basis_weights(received, node_positions, tile_lists):
    tile_count = tile_lists.shape[0]
    tile_width = received.shape[2]
    chosen = received[tile_lists]
    nodes_at = node_positions.reshape(3, tile_count, tile_width)
    distance = jnp.zeros((tile_count, tile_width, tile_lists.shape[1], tile_width), jnp.float32)
    for component in range(3):
        offset = nodes_at[component][:, :, None, None] - chosen[:, None, :, 3 + component, :]
        distance = distance + offset * offset
    kernel = 1.0 / jnp.sqrt(1.0 + distance / (basis_radius * basis_radius))
    column = jnp.sum(kernel, axis=1)
    totals = (
        jnp.zeros((received.shape[0], tile_width), jnp.float32)
        .at[tile_lists.reshape(-1)]
        .add(column.reshape(-1, tile_width))
    )
    return (kernel / totals[tile_lists][:, None, :, :], chosen)


def map_tractions(weights, chosen, node_index, nodes_total):
    mapped = jnp.einsum(
        "anbp,abcp->can", weights, chosen[:, :, 0:3, :], precision=lax.Precision.HIGHEST
    )
    return jnp.zeros((3, nodes_total), jnp.float32).at[:, node_index].add(mapped.reshape(3, -1))


def map_speeds(weights, solution_flat, node_index, tile_lists, tile_slots):
    tile_count = weights.shape[0]
    tile_width = weights.shape[1]
    at_nodes = solution_flat[:, node_index].reshape(3, tile_count, tile_width)
    contrib = jnp.einsum("anbp,can->abcp", weights, at_nodes, precision=lax.Precision.HIGHEST)
    return (
        jnp.zeros((tile_slots, 3, tile_width), jnp.float32)
        .at[tile_lists.reshape(-1)]
        .add(contrib.reshape(-1, 3, tile_width))
    )


def element_sum(widened, matrix):
    span_cells = widened.shape[1] - 2
    across_cells = widened.shape[2] - 2
    deep_cells = widened.shape[3]
    widened_z = jnp.pad(widened, ((0, 0), (0, 0), (0, 0), (0, 1)))
    corners = [(a, b, c) for a in (0, 1) for b in (0, 1) for c in (0, 1)]
    gathered = jnp.concatenate(
        [
            widened_z[0:3, a : a + span_cells + 1, b : b + across_cells + 1, c : c + deep_cells]
            for a, b, c in corners
        ],
        axis=0,
    )
    element_scale = widened_z[3, 0 : span_cells + 1, 0 : across_cells + 1, 0:deep_cells]
    forces = element_scale * jnp.einsum(
        "ij,jabc->iabc", matrix, gathered, precision=lax.Precision.HIGHEST
    )
    summed = jnp.zeros((3, span_cells + 2, across_cells + 2, deep_cells + 1), jnp.float32)
    for corner_id, (a, b, c) in enumerate(corners):
        summed = summed.at[
            :, a : a + span_cells + 1, b : b + across_cells + 1, c : c + deep_cells
        ].add(forces[3 * corner_id : 3 * corner_id + 3])
    return summed[:, 1 : span_cells + 1, 1 : across_cells + 1, 0:deep_cells]


def apply_operator(values, stiffness, is_struct, matrix):
    stacked = jnp.concatenate([values, stiffness[None]], axis=0)
    widened = padded(stacked, (("gx", 1), ("gy", 2)), 1)

    def active_side(operands):
        return mass_shift * operands[2] + element_sum(operands[0], operands[1])

    def quiet_side(operands):
        return jnp.zeros_like(operands[2])

    return lax.cond(is_struct, active_side, quiet_side, (widened, matrix, values))


def global_products(first_vec, second_vec):
    return lax.psum(
        (jnp.sum(first_vec * first_vec), jnp.sum(first_vec * second_vec)), ("group", "gx", "gy")
    )


def solve_structure(right_side, operator, products):
    residual = right_side
    image_vec = operator(residual)
    norm_now, curvature = products(residual, image_vec)
    step_size = norm_now / curvature
    direction, image_dir = (residual, image_vec)
    solution = jnp.zeros_like(right_side)
    for iteration in range(ITERS):
        solution = solution + step_size * direction
        residual = residual - step_size * image_dir
        if iteration + 1 < ITERS:
            image_vec = operator(residual)
            norm_next, curvature = products(residual, image_vec)
            beta_ratio = norm_next / norm_now
            step_size = norm_next / (curvature - beta_ratio * norm_next / step_size)
            direction = residual + beta_ratio * direction
            image_dir = image_vec + beta_ratio * image_dir
            norm_now = norm_next
    return solution


def per_device(
    populations,
    solid_mask,
    wall_cells,
    body_load,
    elem_scale,
    elem_active,
    elem_matrix,
    iface_nodes,
    iface_coords,
    neighbours,
):
    group_count = lax.axis_size("group")
    span_devices = lax.axis_size("gx")
    struct_groups = max(1, group_count // 8)
    fluid_groups = group_count - struct_groups
    group_index = lax.axis_index("group")
    slab_index = group_index * span_devices + lax.axis_index("gx")
    column_index = lax.axis_index("gy")
    is_fluid = group_index < fluid_groups
    is_struct = jnp.logical_not(is_fluid)
    span_cells, across_cells, deep_cells = solid_mask.shape
    cell_count = span_cells * across_cells * deep_cells
    fluid_here = jnp.where(is_fluid, 1.0 - solid_mask.astype(jnp.float32), 0.0)
    relaxed_pops = lax.cond(
        is_fluid,
        lambda pops: collide(pops.astype(jnp.float32)).astype(jnp.bfloat16),
        lambda pops: jnp.zeros_like(pops),
        populations,
    )
    marker = fluid_here.astype(jnp.bfloat16)[None]
    widened = padded(
        jnp.concatenate([relaxed_pops, marker], axis=0), ((("group", "gx"), 1), ("gy", 2)), 1
    )
    widened = jnp.pad(widened, ((0, 0), (0, 0), (0, 0), (1, 1))).astype(jnp.float32)
    moved = widened[0:19]
    fluid_ext = widened[19]
    wall_index = wall_cells.reshape(-1)
    point_count = wall_index.shape[0]
    tiles_out = point_count // TILE

    def fluid_pack(operands):
        upstream, opened, bounce, reflected = stream_links(operands[0], operands[1])
        force_parts = wall_force(bounce, reflected).reshape(3, cell_count)
        picked = force_parts[:, wall_index]
        span_pos = wall_index // (across_cells * deep_cells)
        across_pos = wall_index // deep_cells % across_cells + column_index * across_cells
        deep_pos = wall_index % deep_cells
        positions = jnp.stack(
            [
                (slab_index * span_cells + span_pos).astype(jnp.float32),
                across_pos.astype(jnp.float32),
                deep_pos.astype(jnp.float32),
            ]
        )
        packed = jnp.concatenate([picked, positions], axis=0)
        return packed.reshape(6, tiles_out, TILE).transpose(1, 0, 2)

    packed = lax.cond(
        is_fluid,
        fluid_pack,
        lambda operands: jnp.zeros((tiles_out, 6, TILE), jnp.float32),
        (moved, fluid_ext),
    )
    received = lax.all_gather(packed, "group", axis=0, tiled=True)
    node_index = iface_nodes.reshape(-1)
    node_positions = iface_coords.reshape(3, -1)
    tile_lists = neighbours.reshape(neighbours.shape[2], neighbours.shape[3])
    nodes_total = body_load.shape[1] * body_load.shape[2] * body_load.shape[3]
    weight_shape = (tile_lists.shape[0], TILE, tile_lists.shape[1], TILE)

    def struct_map(received_all):
        weights, chosen = basis_weights(received_all, node_positions, tile_lists)
        mapped = map_tractions(weights, chosen, node_index, nodes_total)
        return (weights, body_load + mapped.reshape(body_load.shape))

    def struct_quiet(received_all):
        return (jnp.zeros(weight_shape, jnp.float32), jnp.zeros_like(body_load))

    weights, right_side = lax.cond(is_struct, struct_map, struct_quiet, received)
    stiffness = jnp.where(is_struct, elem_scale * elem_active.astype(jnp.float32), 0.0)
    solution = solve_structure(
        right_side,
        lambda values: apply_operator(values, stiffness, is_struct, elem_matrix),
        global_products,
    )
    tile_slots = received.shape[0]

    def struct_back(operands):
        return map_speeds(
            operands[0], operands[1].reshape(3, nodes_total), node_index, tile_lists, tile_slots
        )

    back_terms = lax.cond(
        is_struct,
        struct_back,
        lambda operands: jnp.zeros((tile_slots, 3, TILE), jnp.float32),
        (weights, solution),
    )
    per_group = tile_slots // group_count
    route_count = fluid_groups // struct_groups
    sender_slot = jnp.clip(group_index - fluid_groups, 0, struct_groups - 1)
    own_speeds = jnp.zeros((per_group, 3, TILE), jnp.float32)
    for route_step in range(route_count):
        offset_row = (sender_slot + route_step * struct_groups) * per_group
        outgoing = lax.dynamic_slice_in_dim(back_terms, offset_row, per_group, 0)
        incoming = passed_along(outgoing, "group", (route_step + 1) * struct_groups)
        own_speeds = own_speeds + jnp.where(
            group_index // struct_groups == route_step, incoming, 0.0
        )
    speed_parts = wall_gain * own_speeds.transpose(1, 0, 2).reshape(3, point_count)
    wall_speed = jnp.zeros((3, cell_count), jnp.float32).at[:, wall_index].add(speed_parts)
    wall_speed = wall_speed.reshape(3, span_cells, across_cells, deep_cells)
    new_populations = lax.cond(
        is_fluid,
        lambda operands: stream_all(operands[0], operands[1], operands[2]),
        lambda operands: jnp.zeros(operands[0][:, 1:-1, 1:-1, 1:-1].shape, jnp.bfloat16),
        (moved, fluid_ext, wall_speed),
    )
    return (new_populations, solution)


def solution(mesh):
    placed = (
        P(None, ("group", "gx"), "gy", None),
        P(("group", "gx"), "gy", None),
        P(("group", "gx"), "gy", None),
        P(None, ("group", "gx"), "gy", None),
        P(("group", "gx"), "gy", None),
        P(("group", "gx"), "gy", None),
        P(),
        P(("group", "gx"), "gy", None),
        P(None, ("group", "gx"), "gy", None),
        P(("group", "gx"), "gy", None, None),
    )
    return jax.shard_map(
        per_device,
        mesh=mesh,
        in_specs=placed,
        out_specs=(P(None, ("group", "gx"), "gy", None), P(None, ("group", "gx"), "gy", None)),
        check_vma=False,
    )
```

profile of v0, /device:TPU:1, one launch (start us, length us, event | category | flops | bytes accessed | tf_op | source)
XLA Modules:
  0.0 306.8 jit_solution(16468863628029610171)
XLA Ops:
  0.7 0.7 fusion.274
  1.4 13.3 %conditional.8 = (bf16[19,2,8,128]{3,2,1,0:T(8,128)(2,1)}) conditional(s32[]{:T(128)} %convert_element_type.59, () %tuple.155, (bf16[19,2,8,128]{3,2,1,0:T(8,128)(2,1)}) %tuple.170), branch_computations={%region_0.1_spmd, %region_1.3_spmd} | conditional | flops 724991 | bytes 1282056 | solution.py:267
  1.4 0.9 convert_element_type.49
  2.3 0.9 convert_reduce_fusion
  14.7 0.8 fusion.271
  15.5 4.0 %collective-permute-start = (bf16[20,1,8,128]{3,2,1,0:T(8,128)(2,1)S(1)}, bf16[20,1,8,128]{3,2,1,0:T(8,128)(2,1)S(1)}, u32[]{:S(2)}, u32[]{:S(2)}) collective-permute-start(bf16[20,1,8,128]{3,2,1,0:T(8,128)(2,1)S(1)} %get-tuple-element.547), channel_id=1, source_target_pairs={{0,2},{2,4},{4,6},{6,8},{8,10},{10,12},{12,14},{14,16},{16,18},{18... | collective-permute-start | bytes 122888 | tf_op jit(solution)/shard_map/ppermute | solution.py:45
  19.5 4.5 %collective-permute-start.1 = (bf16[20,1,8,128]{3,2,1,0:T(8,128)(2,1)S(1)}, bf16[20,1,8,128]{3,2,1,0:T(8,128)(2,1)S(1)}, u32[]{:S(2)}, u32[]{:S(2)}) collective-permute-start(bf16[20,1,8,128]{3,2,1,0:T(8,128)(2,1)S(1)} %get-tuple-element.548), channel_id=1, source_target_pairs={{2,0},{4,2},{6,4},{8,6},{10,8},{12,10},{14,12},{16,14},{18,16},{20... | collective-permute-start | bytes 122888 | tf_op jit(solution)/shard_map/ppermute | solution.py:47
  24.1 1.1 collective-permute-done.1
  25.1 1.0 pad_maximum_fusion.9
  26.2 3.1 %collective-permute-start.2 = (bf16[20,4,1,128]{3,2,1,0:T(2,128)(2,1)S(1)}, bf16[20,4,1,128]{3,2,1,0:T(2,128)(2,1)S(1)}, u32[]{:S(2)}, u32[]{:S(2)}) collective-permute-start(bf16[20,4,1,128]{3,2,1,0:T(2,128)(2,1)S(1)} %get-tuple-element.545), channel_id=1, source_target_pairs={{0,1},{2,3},{4,5},{6,7},{8,9},{10,11},{12,13},{14,15},{16,17},{18,... | collective-permute-start | bytes 61448 | tf_op jit(solution)/shard_map/ppermute | solution.py:45
  29.3 1.3 collective-permute-start.3
  30.6 3.4 %collective-permute-done.3 = bf16[20,4,1,128]{3,2,1,0:T(2,128)(2,1)S(1)} collective-permute-done((bf16[20,4,1,128]{3,2,1,0:T(2,128)(2,1)S(1)}, bf16[20,4,1,128]{3,2,1,0:T(2,128)(2,1)S(1)}, u32[]{:S(2)}, u32[]{:S(2)}) %collective-permute-start.3) | collective-permute-done | bytes 20512 | tf_op jit(solution)/shard_map/ppermute | solution.py:47
  34.0 1.5 fusion.249
  36.2 2.0 conditional.9
  37.0 1.0 gather_fusion
  38.2 7.8 %all_gather.3 = f32[16,6,128]{2,1,0:T(8,128)S(1)} all-gather(f32[4,6,128]{2,1,0:T(8,128)S(1)} %copy.69), channel_id=1, replica_groups=mesh['group'=4,'gx'=4,'gy'=2] {'group'}, dimensions={0}, use_global_device_ids=true | all-gather | bytes 61440 | tf_op jit(solution)/shard_map/all_gather | solution.py:307
  46.0 1.2 conditional.10
  46.1 1.1 broadcast.1066
  47.6 3.2 %collective-permute-start.4 = (f32[4,1,4,128]{3,0,2,1:T(4,128)S(1)}, f32[4,1,4,128]{3,0,2,1:T(4,128)S(1)}, u32[]{:S(2)}, u32[]{:S(2)}) collective-permute-start(f32[4,1,4,128]{3,0,2,1:T(4,128)S(1)} %get-tuple-element.555), channel_id=1, source_target_pairs={{0,2},{2,4},{4,6},{1,3},{3,5},{5,7},{8,10},{10,12},{12,14},{9,11},... | collective-permute-start | bytes 24584 | tf_op jit(solution)/shard_map/ppermute | solution.py:45
  50.8 1.3 collective-permute-start.5
  52.1 3.1 %collective-permute-done.5 = f32[4,1,4,128]{3,0,2,1:T(4,128)S(1)} collective-permute-done((f32[4,1,4,128]{3,0,2,1:T(4,128)S(1)}, f32[4,1,4,128]{3,0,2,1:T(4,128)S(1)}, u32[]{:S(2)}, u32[]{:S(2)}) %collective-permute-start.5) | collective-permute-done | bytes 8224 | tf_op jit(solution)/shard_map/ppermute | solution.py:47
  55.2 1.3 collective-permute-start.6
  56.5 1.3 collective-permute-start.7
  57.8 0.9 multiply_reduce_fusion
  58.7 2.3 collective-permute-done.7
  62.0 65.4 %all-reduce.9 = (f32[]{:T(128)}, f32[]{:T(128)}) all-reduce(f32[]{:T(128)} %multiply_reduce_fusion, f32[]{:T(128)} %multiply_reduce_fusion.1), channel_id=1, replica_groups=mesh['group'=4,'gx'=4,'gy'=2] {'group','gx','gy'}, use_global_device_ids=true, to_apply=%region_11.12 | all-reduce | flops 2 | bytes 16 | tf_op jit(solution)/shard_map/psum | solution.py:217
  128.8 2.1 collective-permute-start.8
  130.9 1.3 collective-permute-start.9
  132.2 3.1 %collective-permute-done.9 = f32[4,1,4,128]{3,2,1,0:T(4,128)S(1)} collective-permute-done((f32[4,1,4,128]{3,2,1,0:T(4,128)S(1)}, f32[4,1,4,128]{3,2,1,0:T(4,128)S(1)}, u32[]{:S(2)}, u32[]{:S(2)}) %collective-permute-start.9) | collective-permute-done | bytes 8224 | tf_op jit(solution)/shard_map/ppermute | solution.py:47
  135.3 2.6 collective-permute-start.10
  137.9 1.3 collective-permute-start.11
  139.2 3.1 %collective-permute-done.11 = f32[4,6,1,128]{3,2,1,0:T(1,128)S(1)} collective-permute-done((f32[4,6,1,128]{3,2,1,0:T(1,128)S(1)}, f32[4,6,1,128]{3,2,1,0:T(1,128)S(1)}, u32[]{:S(2)}, u32[]{:S(2)}) %collective-permute-start.11) | collective-permute-done | bytes 12320 | tf_op jit(solution)/shard_map/ppermute | solution.py:47
  142.6 0.7 multiply_reduce_fusion.4
  143.3 55.8 %all-reduce.8 = (f32[]{:T(128)}, f32[]{:T(128)}) all-reduce(f32[]{:T(128)} %get-tuple-element.478, f32[]{:T(128)} %get-tuple-element.477), channel_id=1, replica_groups=mesh['group'=4,'gx'=4,'gy'=2] {'group','gx','gy'}, use_global_device_ids=true, to_apply=%region_17.18 | all-reduce | flops 2 | bytes 16 | tf_op jit(solution)/shard_map/psum | solution.py:217
  203.7 2.2 collective-permute-start.12
  205.9 1.3 collective-permute-start.13
  207.2 3.1 %collective-permute-done.13 = f32[4,1,4,128]{3,2,1,0:T(4,128)S(1)} collective-permute-done((f32[4,1,4,128]{3,2,1,0:T(4,128)S(1)}, f32[4,1,4,128]{3,2,1,0:T(4,128)S(1)}, u32[]{:S(2)}, u32[]{:S(2)}) %collective-permute-start.13) | collective-permute-done | bytes 8224 | tf_op jit(solution)/shard_map/ppermute | solution.py:47
  210.4 2.5 collective-permute-start.14
  212.9 1.3 collective-permute-start.15
  214.2 3.1 %collective-permute-done.15 = f32[4,6,1,128]{3,2,1,0:T(1,128)S(1)} collective-permute-done((f32[4,6,1,128]{3,2,1,0:T(1,128)S(1)}, f32[4,6,1,128]{3,2,1,0:T(1,128)S(1)}, u32[]{:S(2)}, u32[]{:S(2)}) %collective-permute-start.15) | collective-permute-done | bytes 12320 | tf_op jit(solution)/shard_map/ppermute | solution.py:47
  218.0 55.8 %all-reduce.7 = (f32[]{:T(128)}, f32[]{:T(128)}) all-reduce(f32[]{:T(128)} %get-tuple-element.476, f32[]{:T(128)} %get-tuple-element.475), channel_id=1, replica_groups=mesh['group'=4,'gx'=4,'gy'=2] {'group','gx','gy'}, use_global_device_ids=true, to_apply=%region_23.24 | all-reduce | flops 2 | bytes 16 | tf_op jit(solution)/shard_map/psum | solution.py:217
  279.0 0.7 constant_dynamic-slice_fusion.2
  279.8 3.4 %collective-permute-start.16 = (f32[4,3,128]{2,1,0:T(4,128)S(1)}, f32[4,3,128]{2,1,0:T(4,128)S(1)}, u32[]{:S(2)}, u32[]{:S(2)}) collective-permute-start(f32[4,3,128]{2,1,0:T(4,128)S(1)} %get-tuple-element.557), channel_id=1, source_target_pairs={{0,8},{8,16},{16,24},{24,0},{1,9},{9,17},{17,25},{25,1},{2,10},{10... | collective-permute-start | bytes 18440 | tf_op jit(solution)/shard_map/ppermute | solution.py:57
  283.1 3.3 %collective-permute-start.17 = (f32[4,3,128]{2,1,0:T(4,128)S(1)}, f32[4,3,128]{2,1,0:T(4,128)S(1)}, u32[]{:S(2)}, u32[]{:S(2)}) collective-permute-start(f32[4,3,128]{2,1,0:T(4,128)S(1)} %get-tuple-element.559), channel_id=1, source_target_pairs={{0,16},{8,24},{16,0},{24,8},{1,17},{9,25},{17,1},{25,9},{2,18},{10... | collective-permute-start | bytes 18440 | tf_op jit(solution)/shard_map/ppermute | solution.py:57
  286.4 0.7 collective-permute-start.18
  287.7 1.8 collective-permute-done.18
  289.7 2.5 scatter_custom_fusion.3
  292.2 14.7 %conditional.15 = (bf16[19,2,8,128]{3,2,1,0:T(8,128)(2,1)}) conditional(s32[]{:T(128)} %convert_element_type.59, () %tuple.154, (f32[4,10,130]{2,1,0:T(8,128)S(1)}, f32[19,4,10,130]{3,2,1,0:T(8,128)S(1)}, f32[3,2048]{0,1:T(8,128)S(1)}) %tuple.168), branch_computations={%region_32.33_spmd, %region_33.34_spmd} | conditional | flops 356351 | bytes 1826696 | solution.py:356
  292.2 0.7 slice_bitcast_fusion
  292.9 0.7 constant_dynamic-update-slice_fusion.37
  294.0 1.4 constant_dynamic-update-slice_fusion.36
  295.4 0.7 constant_dynamic-update-slice_fusion.35
  296.1 0.7 constant_dynamic-update-slice_fusion.34
  296.8 0.7 constant_dynamic-update-slice_fusion.33
  298.1 0.7 constant_dynamic-update-slice_fusion.31
  298.8 0.7 constant_dynamic-update-slice_fusion.30
  299.4 0.7 constant_dynamic-update-slice_fusion.29
  300.1 0.7 constant_dynamic-update-slice_fusion.28
  300.8 0.7 constant_dynamic-update-slice_fusion.27
  302.1 0.7 constant_dynamic-update-slice_fusion.25
  302.8 0.7 constant_dynamic-update-slice_fusion.24
  303.5 0.7 constant_dynamic-update-slice_fusion.23
  304.8 0.7 constant_dynamic-update-slice_fusion.21
  305.5 0.7 constant_dynamic-update-slice_fusion.20
  (95 shorter events, 21.1 us)
Async XLA Ops:
  0.6 30.0 %copy-start.3 = (f32[4,4,128]{2,1,0:T(4,128)S(1)}, f32[4,4,128]{2,1,0:T(4,128)}, u32[]{:S(2)}) copy-start(f32[4,4,128]{2,1,0:T(4,128)} %param.78) | copy-start | bytes 24580
  0.6 30.0 %copy-start.4 = (s32[4,4,128]{2,1,0:T(4,128)S(1)}, s32[4,4,128]{2,1,0:T(4,128)}, u32[]{:S(2)}) copy-start(s32[4,4,128]{2,1,0:T(4,128)} %param.79) | copy-start | bytes 24580
  15.5 8.6 %collective-permute-start = (bf16[20,1,8,128]{3,2,1,0:T(8,128)(2,1)S(1)}, bf16[20,1,8,128]{3,2,1,0:T(8,128)(2,1)S(1)}, u32[]{:S(2)}, u32[]{:S(2)}) collective-permute-start(bf16[20,1,8,128]{3,2,1,0:T(8,128)(2,1)S(1)} %get-tuple-element.547), channel_id=1, source_target_pairs={{0,2},{2,4},{4,6},{6,8},{8,10},{10,12},{12,14},{14,16},{16,18},{18... | collective-permute-start | bytes 122888 | tf_op jit(solution)/shard_map/ppermute | solution.py:45
  19.5 5.6 %collective-permute-start.1 = (bf16[20,1,8,128]{3,2,1,0:T(8,128)(2,1)S(1)}, bf16[20,1,8,128]{3,2,1,0:T(8,128)(2,1)S(1)}, u32[]{:S(2)}, u32[]{:S(2)}) collective-permute-start(bf16[20,1,8,128]{3,2,1,0:T(8,128)(2,1)S(1)} %get-tuple-element.548), channel_id=1, source_target_pairs={{2,0},{4,2},{6,4},{8,6},{10,8},{12,10},{14,12},{16,14},{18,16},{20... | collective-permute-start | bytes 122888 | tf_op jit(solution)/shard_map/ppermute | solution.py:47
  26.2 4.5 %collective-permute-start.2 = (bf16[20,4,1,128]{3,2,1,0:T(2,128)(2,1)S(1)}, bf16[20,4,1,128]{3,2,1,0:T(2,128)(2,1)S(1)}, u32[]{:S(2)}, u32[]{:S(2)}) collective-permute-start(bf16[20,4,1,128]{3,2,1,0:T(2,128)(2,1)S(1)} %get-tuple-element.545), channel_id=1, source_target_pairs={{0,1},{2,3},{4,5},{6,7},{8,9},{10,11},{12,13},{14,15},{16,17},{18,... | collective-permute-start | bytes 61448 | tf_op jit(solution)/shard_map/ppermute | solution.py:45
  29.3 4.7 %collective-permute-start.3 = (bf16[20,4,1,128]{3,2,1,0:T(2,128)(2,1)S(1)}, bf16[20,4,1,128]{3,2,1,0:T(2,128)(2,1)S(1)}, u32[]{:S(2)}, u32[]{:S(2)}) collective-permute-start(bf16[20,4,1,128]{3,2,1,0:T(2,128)(2,1)S(1)} %get-tuple-element.546), channel_id=1, source_target_pairs={{1,0},{3,2},{5,4},{7,6},{9,8},{11,10},{13,12},{15,14},{17,16},{19,... | collective-permute-start | bytes 61448 | tf_op jit(solution)/shard_map/ppermute | solution.py:47
  35.6 0.7 copy-start.2
  35.7 10.3 %copy-start.1 = (f32[3,4,4,128]{3,2,1,0:T(4,128)S(1)}, f32[3,4,4,128]{3,2,1,0:T(4,128)}, u32[]{:S(2)}) copy-start(f32[3,4,4,128]{3,2,1,0:T(4,128)} %param.77) | copy-start | bytes 73732
  35.7 10.3 %copy-start.5 = (s32[1,1,256]{2,1,0:T(1,128)S(1)}, s32[1,1,256]{2,1,0:T(1,128)}, u32[]{:S(2)}) copy-start(s32[1,1,256]{2,1,0:T(1,128)} %param.81) | copy-start | bytes 3076
  35.7 10.3 %copy-start.6 = (f32[3,1,1,256]{3,2,1,0:T(1,128)S(1)}, f32[3,1,1,256]{3,2,1,0:T(1,128)}, u32[]{:S(2)}) copy-start(f32[3,1,1,256]{3,2,1,0:T(1,128)} %param.82) | copy-start | bytes 9220
  35.7 10.3 %copy-start.7 = (s32[1,1,2,8]{3,2,1,0:T(2,128)S(1)}, s32[1,1,2,8]{3,2,1,0:T(2,128)}, u32[]{:S(2)}) copy-start(s32[1,1,2,8]{3,2,1,0:T(2,128)} %param.83) | copy-start | bytes 196
  47.3 13.8 %copy-start = (f32[24,24]{1,0:T(8,128)S(1)}, f32[24,24]{1,0:T(8,128)}, u32[]{:S(2)}) copy-start(f32[24,24]{1,0:T(8,128)} %param.80) | copy-start | bytes 6916
  47.6 4.5 %collective-permute-start.4 = (f32[4,1,4,128]{3,0,2,1:T(4,128)S(1)}, f32[4,1,4,128]{3,0,2,1:T(4,128)S(1)}, u32[]{:S(2)}, u32[]{:S(2)}) collective-permute-start(f32[4,1,4,128]{3,0,2,1:T(4,128)S(1)} %get-tuple-element.555), channel_id=1, source_target_pairs={{0,2},{2,4},{4,6},{1,3},{3,5},{5,7},{8,10},{10,12},{12,14},{9,11},... | collective-permute-start | bytes 24584 | tf_op jit(solution)/shard_map/ppermute | solution.py:45
  50.8 4.4 %collective-permute-start.5 = (f32[4,1,4,128]{3,0,2,1:T(4,128)S(1)}, f32[4,1,4,128]{3,0,2,1:T(4,128)S(1)}, u32[]{:S(2)}, u32[]{:S(2)}) collective-permute-start(f32[4,1,4,128]{3,0,2,1:T(4,128)S(1)} %get-tuple-element.556), channel_id=1, source_target_pairs={{2,0},{4,2},{6,4},{3,1},{5,3},{7,5},{10,8},{12,10},{14,12},{11,9},... | collective-permute-start | bytes 24584 | tf_op jit(solution)/shard_map/ppermute | solution.py:47
  55.2 3.5 %collective-permute-start.6 = (f32[4,6,1,128]{3,0,2,1:T(4,128)S(1)}, f32[4,6,1,128]{3,0,2,1:T(4,128)S(1)}, u32[]{:S(2)}, u32[]{:S(2)}) collective-permute-start(f32[4,6,1,128]{3,0,2,1:T(4,128)S(1)} %get-tuple-element.549), channel_id=1, source_target_pairs={{0,1},{2,3},{4,5},{6,7},{8,9},{10,11},{12,13},{14,15},{16,17},{18,... | collective-permute-start | bytes 36872 | tf_op jit(solution)/shard_map/ppermute | solution.py:45
  56.5 4.4 %collective-permute-start.7 = (f32[4,6,1,128]{3,0,2,1:T(4,128)S(1)}, f32[4,6,1,128]{3,0,2,1:T(4,128)S(1)}, u32[]{:S(2)}, u32[]{:S(2)}) collective-permute-start(f32[4,6,1,128]{3,0,2,1:T(4,128)S(1)} %get-tuple-element.550), channel_id=1, source_target_pairs={{1,0},{3,2},{5,4},{7,6},{9,8},{11,10},{13,12},{15,14},{17,16},{19,... | collective-permute-start | bytes 36872 | tf_op jit(solution)/shard_map/ppermute | solution.py:47
  128.8 3.4 %collective-permute-start.8 = (f32[4,1,4,128]{3,2,1,0:T(4,128)S(1)}, f32[4,1,4,128]{3,2,1,0:T(4,128)S(1)}, u32[]{:S(2)}, u32[]{:S(2)}) collective-permute-start(f32[4,1,4,128]{3,2,1,0:T(4,128)S(1)} %get-tuple-element.562), channel_id=1, source_target_pairs={{0,2},{2,4},{4,6},{1,3},{3,5},{5,7},{8,10},{10,12},{12,14},{9,11},... | collective-permute-start | bytes 24584 | tf_op jit(solution)/shard_map/ppermute | solution.py:45
  130.9 4.4 %collective-permute-start.9 = (f32[4,1,4,128]{3,2,1,0:T(4,128)S(1)}, f32[4,1,4,128]{3,2,1,0:T(4,128)S(1)}, u32[]{:S(2)}, u32[]{:S(2)}) collective-permute-start(f32[4,1,4,128]{3,2,1,0:T(4,128)S(1)} %get-tuple-element.563), channel_id=1, source_target_pairs={{2,0},{4,2},{6,4},{3,1},{5,3},{7,5},{10,8},{12,10},{14,12},{11,9},... | collective-permute-start | bytes 24584 | tf_op jit(solution)/shard_map/ppermute | solution.py:47
  135.3 3.9 %collective-permute-start.10 = (f32[4,6,1,128]{3,2,1,0:T(1,128)S(1)}, f32[4,6,1,128]{3,2,1,0:T(1,128)S(1)}, u32[]{:S(2)}, u32[]{:S(2)}) collective-permute-start(f32[4,6,1,128]{3,2,1,0:T(1,128)S(1)} %get-tuple-element.553), channel_id=1, source_target_pairs={{0,1},{2,3},{4,5},{6,7},{8,9},{10,11},{12,13},{14,15},{16,17},{18,... | collective-permute-start | bytes 36872 | tf_op jit(solution)/shard_map/ppermute | solution.py:45
  137.9 4.4 %collective-permute-start.11 = (f32[4,6,1,128]{3,2,1,0:T(1,128)S(1)}, f32[4,6,1,128]{3,2,1,0:T(1,128)S(1)}, u32[]{:S(2)}, u32[]{:S(2)}) collective-permute-start(f32[4,6,1,128]{3,2,1,0:T(1,128)S(1)} %get-tuple-element.554), channel_id=1, source_target_pairs={{1,0},{3,2},{5,4},{7,6},{9,8},{11,10},{13,12},{15,14},{17,16},{19,... | collective-permute-start | bytes 36872 | tf_op jit(solution)/shard_map/ppermute | solution.py:47
  203.7 3.5 %collective-permute-start.12 = (f32[4,1,4,128]{3,2,1,0:T(4,128)S(1)}, f32[4,1,4,128]{3,2,1,0:T(4,128)S(1)}, u32[]{:S(2)}, u32[]{:S(2)}) collective-permute-start(f32[4,1,4,128]{3,2,1,0:T(4,128)S(1)} %get-tuple-element.560), channel_id=1, source_target_pairs={{0,2},{2,4},{4,6},{1,3},{3,5},{5,7},{8,10},{10,12},{12,14},{9,11},... | collective-permute-start | bytes 24584 | tf_op jit(solution)/shard_map/ppermute | solution.py:45
  205.9 4.4 %collective-permute-start.13 = (f32[4,1,4,128]{3,2,1,0:T(4,128)S(1)}, f32[4,1,4,128]{3,2,1,0:T(4,128)S(1)}, u32[]{:S(2)}, u32[]{:S(2)}) collective-permute-start(f32[4,1,4,128]{3,2,1,0:T(4,128)S(1)} %get-tuple-element.561), channel_id=1, source_target_pairs={{2,0},{4,2},{6,4},{3,1},{5,3},{7,5},{10,8},{12,10},{14,12},{11,9},... | collective-permute-start | bytes 24584 | tf_op jit(solution)/shard_map/ppermute | solution.py:47
  210.4 3.8 %collective-permute-start.14 = (f32[4,6,1,128]{3,2,1,0:T(1,128)S(1)}, f32[4,6,1,128]{3,2,1,0:T(1,128)S(1)}, u32[]{:S(2)}, u32[]{:S(2)}) collective-permute-start(f32[4,6,1,128]{3,2,1,0:T(1,128)S(1)} %get-tuple-element.551), channel_id=1, source_target_pairs={{0,1},{2,3},{4,5},{6,7},{8,9},{10,11},{12,13},{14,15},{16,17},{18,... | collective-permute-start | bytes 36872 | tf_op jit(solution)/shard_map/ppermute | solution.py:45
  212.9 4.4 %collective-permute-start.15 = (f32[4,6,1,128]{3,2,1,0:T(1,128)S(1)}, f32[4,6,1,128]{3,2,1,0:T(1,128)S(1)}, u32[]{:S(2)}, u32[]{:S(2)}) collective-permute-start(f32[4,6,1,128]{3,2,1,0:T(1,128)S(1)} %get-tuple-element.552), channel_id=1, source_target_pairs={{1,0},{3,2},{5,4},{7,6},{9,8},{11,10},{13,12},{15,14},{17,16},{19,... | collective-permute-start | bytes 36872 | tf_op jit(solution)/shard_map/ppermute | solution.py:47
  279.8 7.4 %collective-permute-start.16 = (f32[4,3,128]{2,1,0:T(4,128)S(1)}, f32[4,3,128]{2,1,0:T(4,128)S(1)}, u32[]{:S(2)}, u32[]{:S(2)}) collective-permute-start(f32[4,3,128]{2,1,0:T(4,128)S(1)} %get-tuple-element.557), channel_id=1, source_target_pairs={{0,8},{8,16},{16,24},{24,0},{1,9},{9,17},{17,25},{25,1},{2,10},{10... | collective-permute-start | bytes 18440 | tf_op jit(solution)/shard_map/ppermute | solution.py:57
  283.1 4.5 %collective-permute-start.17 = (f32[4,3,128]{2,1,0:T(4,128)S(1)}, f32[4,3,128]{2,1,0:T(4,128)S(1)}, u32[]{:S(2)}, u32[]{:S(2)}) collective-permute-start(f32[4,3,128]{2,1,0:T(4,128)S(1)} %get-tuple-element.559), channel_id=1, source_target_pairs={{0,16},{8,24},{16,0},{24,8},{1,17},{9,25},{17,1},{25,9},{2,18},{10... | collective-permute-start | bytes 18440 | tf_op jit(solution)/shard_map/ppermute | solution.py:57
  286.4 3.1 %collective-permute-start.18 = (f32[4,3,128]{2,1,0:T(4,128)S(1)}, f32[4,3,128]{2,1,0:T(4,128)S(1)}, u32[]{:S(2)}, u32[]{:S(2)}) collective-permute-start(f32[4,3,128]{2,1,0:T(4,128)S(1)} %get-tuple-element.558), channel_id=1, source_target_pairs={{0,24},{8,0},{16,8},{24,16},{1,25},{9,1},{17,9},{25,17},{2,26},{10... | collective-permute-start | bytes 18440 | tf_op jit(solution)/shard_map/ppermute | solution.py:57
where the time goes:
time: 308 us; the launch traced here: 307 us
  blocking collectives  185 us (60%)
  starting transfers between devices  41.9 us (14%)
  other arithmetic  37.4 us (12%)
  waiting for transfers between devices  24.6 us (8%)
  between operations  11 us (4%)
  local copies, waits for them, and re-layouts  6.67 us (2%)
    psum x3, blocking collectives, global_products(): lax.psum((jnp.sum(first_vec * first_vec), jnp.sum(first_vec * second_vec)...  177 us
    cond x36, other arithmetic  23.8 us
    ppermute x8, waiting for transfers between devices, padded(): lax.ppermute(head, axis, [((i + 1) % count, i) for i in range(ends)])  22.2 us
    ppermute x8, starting transfers between devices, padded(): lax.ppermute(tail, axis, [(i, (i + 1) % count) for i in range(ends)])  21 us
    ppermute x8, starting transfers between devices, padded(): lax.ppermute(head, axis, [((i + 1) % count, i) for i in range(ends)])  13.6 us
    all_gather x1, blocking collectives, per_device(): received = lax.all_gather(packed, 'group', axis=0, tiled=True)  7.8 us
    ppermute x3, starting transfers between devices, passed_along(): return lax.ppermute(value, axis, pairs)  7.38 us
  transfers between devices with their start and end apart: 19, of which 10 were waited for; matrix products, arithmetic and copies ran while one was open for 0% of the time, Pallas kernels for 0%

commit v1 on v0

--- a/solution.py
+++ b/solution.py
@@ -215,7 +215,8 @@
 
 def global_products(first_vec, second_vec):
     return lax.psum(
-        (jnp.sum(first_vec * first_vec), jnp.sum(first_vec * second_vec)), ("group", "gx", "gy")
+        lax.psum((jnp.sum(first_vec * first_vec), jnp.sum(first_vec * second_vec)), ("gx", "gy")),
+        "group",
     )
 
 

time: 308 us -> 254 us (0.82)
  blocking collectives: 185 us -> 131 us
    psum x3, blocking collectives: 177 us -> 44.2 us  [global_products(): lax.psum((jnp.sum(first_vec * first_vec), jnp.sum(first_vec * second_vec)...]
    psum x0 -> x3, blocking collectives: none -> 78.7 us  [global_products(): lax.psum(lax.psum((jnp.sum(first_vec * first_vec), jnp.sum(first_vec * se...]
where the time goes in v1:
time: 254 us; the launch traced here: 253 us
  blocking collectives  131 us (52%)
  starting transfers between devices  41.6 us (16%)
  other arithmetic  37.4 us (15%)
  waiting for transfers between devices  24.6 us (10%)
  between operations  11.1 us (4%)
  local copies, waits for them, and re-layouts  6.64 us (3%)
    psum x3, blocking collectives, global_products(): lax.psum(lax.psum((jnp.sum(first_vec * first_vec), jnp.sum(first_vec * se...  78.7 us
    psum x3, blocking collectives, global_products(): lax.psum((jnp.sum(first_vec * first_vec), jnp.sum(first_vec * second_vec)...  44.2 us
    cond x36, other arithmetic  23.8 us
    ppermute x8, waiting for transfers between devices, padded(): lax.ppermute(head, axis, [((i + 1) % count, i) for i in range(ends)])  22.2 us
    ppermute x8, starting transfers between devices, padded(): lax.ppermute(tail, axis, [(i, (i + 1) % count) for i in range(ends)])  20 us
    ppermute x8, starting transfers between devices, padded(): lax.ppermute(head, axis, [((i + 1) % count, i) for i in range(ends)])  13.6 us
    ppermute x3, starting transfers between devices, passed_along(): return lax.ppermute(value, axis, pairs)  8.14 us
    all_gather x1, blocking collectives, per_device(): received = lax.all_gather(packed, 'group', axis=0, tiled=True)  7.8 us
  transfers between devices with their start and end apart: 19, of which 10 were waited for; matrix products, arithmetic and copies ran while one was open for 0% of the time, Pallas kernels for 0%

profile of v1, /device:TPU:1, one launch (start us, length us, event | category | flops | bytes accessed | tf_op | source)
XLA Modules:
  0.0 252.5 jit_solution(17072028223877614657)
XLA Ops:
  0.7 0.7 fusion.274
  1.4 13.3 %conditional.8 = (bf16[19,2,8,128]{3,2,1,0:T(8,128)(2,1)}) conditional(s32[]{:T(128)} %convert_element_type.59, () %tuple.155, (bf16[19,2,8,128]{3,2,1,0:T(8,128)(2,1)}) %tuple.170), branch_computations={%region_0.1_spmd, %region_1.3_spmd} | conditional | flops 724991 | bytes 1282056 | solution.py:268
  1.4 0.9 convert_element_type.49
  2.3 0.9 convert_reduce_fusion
  14.7 0.8 fusion.271
  15.5 4.0 %collective-permute-start = (bf16[20,1,8,128]{3,2,1,0:T(8,128)(2,1)S(1)}, bf16[20,1,8,128]{3,2,1,0:T(8,128)(2,1)S(1)}, u32[]{:S(2)}, u32[]{:S(2)}) collective-permute-start(bf16[20,1,8,128]{3,2,1,0:T(8,128)(2,1)S(1)} %get-tuple-element.553), channel_id=1, source_target_pairs={{0,2},{2,4},{4,6},{6,8},{8,10},{10,12},{12,14},{14,16},{16,18},{18... | collective-permute-start | bytes 122888 | tf_op jit(solution)/shard_map/ppermute | solution.py:45
  19.5 4.5 %collective-permute-start.1 = (bf16[20,1,8,128]{3,2,1,0:T(8,128)(2,1)S(1)}, bf16[20,1,8,128]{3,2,1,0:T(8,128)(2,1)S(1)}, u32[]{:S(2)}, u32[]{:S(2)}) collective-permute-start(bf16[20,1,8,128]{3,2,1,0:T(8,128)(2,1)S(1)} %get-tuple-element.554), channel_id=1, source_target_pairs={{2,0},{4,2},{6,4},{8,6},{10,8},{12,10},{14,12},{16,14},{18,16},{20... | collective-permute-start | bytes 122888 | tf_op jit(solution)/shard_map/ppermute | solution.py:47
  24.1 1.1 collective-permute-done.1
  25.1 1.0 pad_maximum_fusion.9
  26.2 3.1 %collective-permute-start.2 = (bf16[20,4,1,128]{3,2,1,0:T(2,128)(2,1)S(1)}, bf16[20,4,1,128]{3,2,1,0:T(2,128)(2,1)S(1)}, u32[]{:S(2)}, u32[]{:S(2)}) collective-permute-start(bf16[20,4,1,128]{3,2,1,0:T(2,128)(2,1)S(1)} %get-tuple-element.551), channel_id=1, source_target_pairs={{0,1},{2,3},{4,5},{6,7},{8,9},{10,11},{12,13},{14,15},{16,17},{18,... | collective-permute-start | bytes 61448 | tf_op jit(solution)/shard_map/ppermute | solution.py:45
  29.3 1.3 collective-permute-start.3
  30.6 3.4 %collective-permute-done.3 = bf16[20,4,1,128]{3,2,1,0:T(2,128)(2,1)S(1)} collective-permute-done((bf16[20,4,1,128]{3,2,1,0:T(2,128)(2,1)S(1)}, bf16[20,4,1,128]{3,2,1,0:T(2,128)(2,1)S(1)}, u32[]{:S(2)}, u32[]{:S(2)}) %collective-permute-start.3) | collective-permute-done | bytes 20512 | tf_op jit(solution)/shard_map/ppermute | solution.py:47
  34.0 1.5 fusion.249
  36.2 2.0 conditional.9
  37.0 1.0 gather_fusion
  38.2 7.8 %all_gather.3 = f32[16,6,128]{2,1,0:T(8,128)S(1)} all-gather(f32[4,6,128]{2,1,0:T(8,128)S(1)} %copy.69), channel_id=1, replica_groups=mesh['group'=4,'gx'=4,'gy'=2] {'group'}, dimensions={0}, use_global_device_ids=true | all-gather | bytes 61440 | tf_op jit(solution)/shard_map/all_gather | solution.py:308
  46.0 1.2 conditional.10
  46.1 1.1 broadcast.1066
  47.6 3.2 %collective-permute-start.4 = (f32[4,1,4,128]{3,0,2,1:T(4,128)S(1)}, f32[4,1,4,128]{3,0,2,1:T(4,128)S(1)}, u32[]{:S(2)}, u32[]{:S(2)}) collective-permute-start(f32[4,1,4,128]{3,0,2,1:T(4,128)S(1)} %get-tuple-element.561), channel_id=1, source_target_pairs={{0,2},{2,4},{4,6},{1,3},{3,5},{5,7},{8,10},{10,12},{12,14},{9,11},... | collective-permute-start | bytes 24584 | tf_op jit(solution)/shard_map/ppermute | solution.py:45
  50.8 1.3 collective-permute-start.5
  52.1 3.1 %collective-permute-done.5 = f32[4,1,4,128]{3,0,2,1:T(4,128)S(1)} collective-permute-done((f32[4,1,4,128]{3,0,2,1:T(4,128)S(1)}, f32[4,1,4,128]{3,0,2,1:T(4,128)S(1)}, u32[]{:S(2)}, u32[]{:S(2)}) %collective-permute-start.5) | collective-permute-done | bytes 8224 | tf_op jit(solution)/shard_map/ppermute | solution.py:47
  55.2 1.3 collective-permute-start.6
  56.5 1.3 collective-permute-start.7
  57.8 0.9 multiply_reduce_fusion
  58.7 2.3 collective-permute-done.7
  62.0 15.3 %all-reduce.9 = (f32[]{:T(128)}, f32[]{:T(128)}) all-reduce(f32[]{:T(128)} %multiply_reduce_fusion, f32[]{:T(128)} %multiply_reduce_fusion.1), channel_id=1, replica_groups=mesh['group'=4,'gx'=4,'gy'=2] {'gx','gy'}, use_global_device_ids=true, to_apply=%region_11.12 | all-reduce | flops 2 | bytes 16 | tf_op jit(solution)/shard_map/psum | solution.py:218
  77.3 32.7 %all-reduce.12 = (f32[]{:T(128)}, f32[]{:T(128)}) all-reduce(f32[]{:T(128)} %get-tuple-element.483, f32[]{:T(128)} %get-tuple-element.484), channel_id=1, replica_groups=mesh['group'=4,'gx'=4,'gy'=2] {'group'}, use_global_device_ids=true, to_apply=%region_12.13 | all-reduce | flops 2 | bytes 16 | tf_op jit(solution)/shard_map/psum | solution.py:217
  111.4 1.3 collective-permute-start.8
  112.7 1.3 collective-permute-start.9
  114.0 3.1 %collective-permute-done.9 = f32[4,1,4,128]{3,2,1,0:T(4,128)S(1)} collective-permute-done((f32[4,1,4,128]{3,2,1,0:T(4,128)S(1)}, f32[4,1,4,128]{3,2,1,0:T(4,128)S(1)}, u32[]{:S(2)}, u32[]{:S(2)}) %collective-permute-start.9) | collective-permute-done | bytes 8224 | tf_op jit(solution)/shard_map/ppermute | solution.py:47
  117.1 2.5 collective-permute-start.10
  119.6 1.3 collective-permute-start.11
  121.0 3.1 %collective-permute-done.11 = f32[4,6,1,128]{3,2,1,0:T(1,128)S(1)} collective-permute-done((f32[4,6,1,128]{3,2,1,0:T(1,128)S(1)}, f32[4,6,1,128]{3,2,1,0:T(1,128)S(1)}, u32[]{:S(2)}, u32[]{:S(2)}) %collective-permute-start.11) | collective-permute-done | bytes 12320 | tf_op jit(solution)/shard_map/ppermute | solution.py:47
  124.3 0.7 multiply_reduce_fusion.4
  125.0 14.5 %all-reduce.8 = (f32[]{:T(128)}, f32[]{:T(128)}) all-reduce(f32[]{:T(128)} %get-tuple-element.478, f32[]{:T(128)} %get-tuple-element.477), channel_id=1, replica_groups=mesh['group'=4,'gx'=4,'gy'=2] {'gx','gy'}, use_global_device_ids=true, to_apply=%region_19.20 | all-reduce | flops 2 | bytes 16 | tf_op jit(solution)/shard_map/psum | solution.py:218
  139.5 23.0 %all-reduce.11 = (f32[]{:T(128)}, f32[]{:T(128)}) all-reduce(f32[]{:T(128)} %get-tuple-element.481, f32[]{:T(128)} %get-tuple-element.482), channel_id=1, replica_groups=mesh['group'=4,'gx'=4,'gy'=2] {'group'}, use_global_device_ids=true, to_apply=%region_20.21 | all-reduce | flops 2 | bytes 16 | tf_op jit(solution)/shard_map/psum | solution.py:217
  167.2 1.3 collective-permute-start.12
  168.5 1.3 collective-permute-start.13
  169.8 3.1 %collective-permute-done.13 = f32[4,1,4,128]{3,2,1,0:T(4,128)S(1)} collective-permute-done((f32[4,1,4,128]{3,2,1,0:T(4,128)S(1)}, f32[4,1,4,128]{3,2,1,0:T(4,128)S(1)}, u32[]{:S(2)}, u32[]{:S(2)}) %collective-permute-start.13) | collective-permute-done | bytes 8224 | tf_op jit(solution)/shard_map/ppermute | solution.py:47
  172.9 3.2 %collective-permute-start.14 = (f32[4,6,1,128]{3,2,1,0:T(1,128)S(1)}, f32[4,6,1,128]{3,2,1,0:T(1,128)S(1)}, u32[]{:S(2)}, u32[]{:S(2)}) collective-permute-start(f32[4,6,1,128]{3,2,1,0:T(1,128)S(1)} %get-tuple-element.557), channel_id=1, source_target_pairs={{0,1},{2,3},{4,5},{6,7},{8,9},{10,11},{12,13},{14,15},{16,17},{18,... | collective-permute-start | bytes 36872 | tf_op jit(solution)/shard_map/ppermute | solution.py:45
  176.2 1.3 collective-permute-start.15
  177.5 3.1 %collective-permute-done.15 = f32[4,6,1,128]{3,2,1,0:T(1,128)S(1)} collective-permute-done((f32[4,6,1,128]{3,2,1,0:T(1,128)S(1)}, f32[4,6,1,128]{3,2,1,0:T(1,128)S(1)}, u32[]{:S(2)}, u32[]{:S(2)}) %collective-permute-start.15) | collective-permute-done | bytes 12320 | tf_op jit(solution)/shard_map/ppermute | solution.py:47
  181.3 14.4 %all-reduce.7 = (f32[]{:T(128)}, f32[]{:T(128)}) all-reduce(f32[]{:T(128)} %get-tuple-element.476, f32[]{:T(128)} %get-tuple-element.475), channel_id=1, replica_groups=mesh['group'=4,'gx'=4,'gy'=2] {'gx','gy'}, use_global_device_ids=true, to_apply=%region_27.28 | all-reduce | flops 2 | bytes 16 | tf_op jit(solution)/shard_map/psum | solution.py:218
  195.7 23.0 %all-reduce.10 = (f32[]{:T(128)}, f32[]{:T(128)}) all-reduce(f32[]{:T(128)} %get-tuple-element.479, f32[]{:T(128)} %get-tuple-element.480), channel_id=1, replica_groups=mesh['group'=4,'gx'=4,'gy'=2] {'group'}, use_global_device_ids=true, to_apply=%region_28.29 | all-reduce | flops 2 | bytes 16 | tf_op jit(solution)/shard_map/psum | solution.py:217
  224.0 0.7 constant_dynamic-slice_fusion.2
  224.7 2.3 collective-permute-start.16
  227.0 5.1 %collective-permute-start.17 = (f32[4,3,128]{2,1,0:T(4,128)S(1)}, f32[4,3,128]{2,1,0:T(4,128)S(1)}, u32[]{:S(2)}, u32[]{:S(2)}) collective-permute-start(f32[4,3,128]{2,1,0:T(4,128)S(1)} %get-tuple-element.565), channel_id=1, source_target_pairs={{0,16},{8,24},{16,0},{24,8},{1,17},{9,25},{17,1},{25,9},{2,18},{10... | collective-permute-start | bytes 18440 | tf_op jit(solution)/shard_map/ppermute | solution.py:57
  232.1 0.7 collective-permute-start.18
  233.4 1.8 collective-permute-done.18
  235.3 2.5 scatter_custom_fusion.3
  237.9 14.7 %conditional.15 = (bf16[19,2,8,128]{3,2,1,0:T(8,128)(2,1)}) conditional(s32[]{:T(128)} %convert_element_type.59, () %tuple.154, (f32[4,10,130]{2,1,0:T(8,128)S(1)}, f32[19,4,10,130]{3,2,1,0:T(8,128)S(1)}, f32[3,2048]{0,1:T(8,128)S(1)}) %tuple.168), branch_computations={%region_38.39_spmd, %region_39.40_spmd} | conditional | flops 356351 | bytes 1826696 | solution.py:357
  237.9 0.7 slice_bitcast_fusion
  238.6 0.7 constant_dynamic-update-slice_fusion.37
  239.6 1.4 constant_dynamic-update-slice_fusion.36
  241.1 0.7 constant_dynamic-update-slice_fusion.35
  241.8 0.7 constant_dynamic-update-slice_fusion.34
  242.4 0.7 constant_dynamic-update-slice_fusion.33
  243.8 0.7 constant_dynamic-update-slice_fusion.31
  244.4 0.7 constant_dynamic-update-slice_fusion.30
  245.1 0.7 constant_dynamic-update-slice_fusion.29
  245.8 0.7 constant_dynamic-update-slice_fusion.28
  246.5 0.7 constant_dynamic-update-slice_fusion.27
  247.8 0.7 constant_dynamic-update-slice_fusion.25
  251.2 0.7 constant_dynamic-update-slice_fusion.20
  (98 shorter events, 23.2 us)
Async XLA Ops:
  0.6 30.0 %copy-start.3 = (f32[4,4,128]{2,1,0:T(4,128)S(1)}, f32[4,4,128]{2,1,0:T(4,128)}, u32[]{:S(2)}) copy-start(f32[4,4,128]{2,1,0:T(4,128)} %param.78) | copy-start | bytes 24580
  0.6 30.0 %copy-start.4 = (s32[4,4,128]{2,1,0:T(4,128)S(1)}, s32[4,4,128]{2,1,0:T(4,128)}, u32[]{:S(2)}) copy-start(s32[4,4,128]{2,1,0:T(4,128)} %param.79) | copy-start | bytes 24580
  15.5 8.6 %collective-permute-start = (bf16[20,1,8,128]{3,2,1,0:T(8,128)(2,1)S(1)}, bf16[20,1,8,128]{3,2,1,0:T(8,128)(2,1)S(1)}, u32[]{:S(2)}, u32[]{:S(2)}) collective-permute-start(bf16[20,1,8,128]{3,2,1,0:T(8,128)(2,1)S(1)} %get-tuple-element.553), channel_id=1, source_target_pairs={{0,2},{2,4},{4,6},{6,8},{8,10},{10,12},{12,14},{14,16},{16,18},{18... | collective-permute-start | bytes 122888 | tf_op jit(solution)/shard_map/ppermute | solution.py:45
  19.5 5.6 %collective-permute-start.1 = (bf16[20,1,8,128]{3,2,1,0:T(8,128)(2,1)S(1)}, bf16[20,1,8,128]{3,2,1,0:T(8,128)(2,1)S(1)}, u32[]{:S(2)}, u32[]{:S(2)}) collective-permute-start(bf16[20,1,8,128]{3,2,1,0:T(8,128)(2,1)S(1)} %get-tuple-element.554), channel_id=1, source_target_pairs={{2,0},{4,2},{6,4},{8,6},{10,8},{12,10},{14,12},{16,14},{18,16},{20... | collective-permute-start | bytes 122888 | tf_op jit(solution)/shard_map/ppermute | solution.py:47
  26.2 4.5 %collective-permute-start.2 = (bf16[20,4,1,128]{3,2,1,0:T(2,128)(2,1)S(1)}, bf16[20,4,1,128]{3,2,1,0:T(2,128)(2,1)S(1)}, u32[]{:S(2)}, u32[]{:S(2)}) collective-permute-start(bf16[20,4,1,128]{3,2,1,0:T(2,128)(2,1)S(1)} %get-tuple-element.551), channel_id=1, source_target_pairs={{0,1},{2,3},{4,5},{6,7},{8,9},{10,11},{12,13},{14,15},{16,17},{18,... | collective-permute-start | bytes 61448 | tf_op jit(solution)/shard_map/ppermute | solution.py:45
  29.3 4.7 %collective-permute-start.3 = (bf16[20,4,1,128]{3,2,1,0:T(2,128)(2,1)S(1)}, bf16[20,4,1,128]{3,2,1,0:T(2,128)(2,1)S(1)}, u32[]{:S(2)}, u32[]{:S(2)}) collective-permute-start(bf16[20,4,1,128]{3,2,1,0:T(2,128)(2,1)S(1)} %get-tuple-element.552), channel_id=1, source_target_pairs={{1,0},{3,2},{5,4},{7,6},{9,8},{11,10},{13,12},{15,14},{17,16},{19,... | collective-permute-start | bytes 61448 | tf_op jit(solution)/shard_map/ppermute | solution.py:47
  35.6 0.7 copy-start.2
  35.7 10.3 %copy-start.1 = (f32[3,4,4,128]{3,2,1,0:T(4,128)S(1)}, f32[3,4,4,128]{3,2,1,0:T(4,128)}, u32[]{:S(2)}) copy-start(f32[3,4,4,128]{3,2,1,0:T(4,128)} %param.77) | copy-start | bytes 73732
  35.7 10.3 %copy-start.5 = (s32[1,1,256]{2,1,0:T(1,128)S(1)}, s32[1,1,256]{2,1,0:T(1,128)}, u32[]{:S(2)}) copy-start(s32[1,1,256]{2,1,0:T(1,128)} %param.81) | copy-start | bytes 3076
  35.7 10.3 %copy-start.6 = (f32[3,1,1,256]{3,2,1,0:T(1,128)S(1)}, f32[3,1,1,256]{3,2,1,0:T(1,128)}, u32[]{:S(2)}) copy-start(f32[3,1,1,256]{3,2,1,0:T(1,128)} %param.82) | copy-start | bytes 9220
  35.8 10.3 %copy-start.7 = (s32[1,1,2,8]{3,2,1,0:T(2,128)S(1)}, s32[1,1,2,8]{3,2,1,0:T(2,128)}, u32[]{:S(2)}) copy-start(s32[1,1,2,8]{3,2,1,0:T(2,128)} %param.83) | copy-start | bytes 196
  47.3 13.8 %copy-start = (f32[24,24]{1,0:T(8,128)S(1)}, f32[24,24]{1,0:T(8,128)}, u32[]{:S(2)}) copy-start(f32[24,24]{1,0:T(8,128)} %param.80) | copy-start | bytes 6916
  47.6 4.5 %collective-permute-start.4 = (f32[4,1,4,128]{3,0,2,1:T(4,128)S(1)}, f32[4,1,4,128]{3,0,2,1:T(4,128)S(1)}, u32[]{:S(2)}, u32[]{:S(2)}) collective-permute-start(f32[4,1,4,128]{3,0,2,1:T(4,128)S(1)} %get-tuple-element.561), channel_id=1, source_target_pairs={{0,2},{2,4},{4,6},{1,3},{3,5},{5,7},{8,10},{10,12},{12,14},{9,11},... | collective-permute-start | bytes 24584 | tf_op jit(solution)/shard_map/ppermute | solution.py:45
  50.8 4.4 %collective-permute-start.5 = (f32[4,1,4,128]{3,0,2,1:T(4,128)S(1)}, f32[4,1,4,128]{3,0,2,1:T(4,128)S(1)}, u32[]{:S(2)}, u32[]{:S(2)}) collective-permute-start(f32[4,1,4,128]{3,0,2,1:T(4,128)S(1)} %get-tuple-element.562), channel_id=1, source_target_pairs={{2,0},{4,2},{6,4},{3,1},{5,3},{7,5},{10,8},{12,10},{14,12},{11,9},... | collective-permute-start | bytes 24584 | tf_op jit(solution)/shard_map/ppermute | solution.py:47
  55.2 3.5 %collective-permute-start.6 = (f32[4,6,1,128]{3,0,2,1:T(4,128)S(1)}, f32[4,6,1,128]{3,0,2,1:T(4,128)S(1)}, u32[]{:S(2)}, u32[]{:S(2)}) collective-permute-start(f32[4,6,1,128]{3,0,2,1:T(4,128)S(1)} %get-tuple-element.555), channel_id=1, source_target_pairs={{0,1},{2,3},{4,5},{6,7},{8,9},{10,11},{12,13},{14,15},{16,17},{18,... | collective-permute-start | bytes 36872 | tf_op jit(solution)/shard_map/ppermute | solution.py:45
  56.5 4.4 %collective-permute-start.7 = (f32[4,6,1,128]{3,0,2,1:T(4,128)S(1)}, f32[4,6,1,128]{3,0,2,1:T(4,128)S(1)}, u32[]{:S(2)}, u32[]{:S(2)}) collective-permute-start(f32[4,6,1,128]{3,0,2,1:T(4,128)S(1)} %get-tuple-element.556), channel_id=1, source_target_pairs={{1,0},{3,2},{5,4},{7,6},{9,8},{11,10},{13,12},{15,14},{17,16},{19,... | collective-permute-start | bytes 36872 | tf_op jit(solution)/shard_map/ppermute | solution.py:47
  111.4 2.6 %collective-permute-start.8 = (f32[4,1,4,128]{3,2,1,0:T(4,128)S(1)}, f32[4,1,4,128]{3,2,1,0:T(4,128)S(1)}, u32[]{:S(2)}, u32[]{:S(2)}) collective-permute-start(f32[4,1,4,128]{3,2,1,0:T(4,128)S(1)} %get-tuple-element.568), channel_id=1, source_target_pairs={{0,2},{2,4},{4,6},{1,3},{3,5},{5,7},{8,10},{10,12},{12,14},{9,11},... | collective-permute-start | bytes 24584 | tf_op jit(solution)/shard_map/ppermute | solution.py:45
  112.7 4.4 %collective-permute-start.9 = (f32[4,1,4,128]{3,2,1,0:T(4,128)S(1)}, f32[4,1,4,128]{3,2,1,0:T(4,128)S(1)}, u32[]{:S(2)}, u32[]{:S(2)}) collective-permute-start(f32[4,1,4,128]{3,2,1,0:T(4,128)S(1)} %get-tuple-element.569), channel_id=1, source_target_pairs={{2,0},{4,2},{6,4},{3,1},{5,3},{7,5},{10,8},{12,10},{14,12},{11,9},... | collective-permute-start | bytes 24584 | tf_op jit(solution)/shard_map/ppermute | solution.py:47
  117.1 3.8 %collective-permute-start.10 = (f32[4,6,1,128]{3,2,1,0:T(1,128)S(1)}, f32[4,6,1,128]{3,2,1,0:T(1,128)S(1)}, u32[]{:S(2)}, u32[]{:S(2)}) collective-permute-start(f32[4,6,1,128]{3,2,1,0:T(1,128)S(1)} %get-tuple-element.559), channel_id=1, source_target_pairs={{0,1},{2,3},{4,5},{6,7},{8,9},{10,11},{12,13},{14,15},{16,17},{18,... | collective-permute-start | bytes 36872 | tf_op jit(solution)/shard_map/ppermute | solution.py:45
  119.6 4.4 %collective-permute-start.11 = (f32[4,6,1,128]{3,2,1,0:T(1,128)S(1)}, f32[4,6,1,128]{3,2,1,0:T(1,128)S(1)}, u32[]{:S(2)}, u32[]{:S(2)}) collective-permute-start(f32[4,6,1,128]{3,2,1,0:T(1,128)S(1)} %get-tuple-element.560), channel_id=1, source_target_pairs={{1,0},{3,2},{5,4},{7,6},{9,8},{11,10},{13,12},{15,14},{17,16},{19,... | collective-permute-start | bytes 36872 | tf_op jit(solution)/shard_map/ppermute | solution.py:47
  167.2 2.6 %collective-permute-start.12 = (f32[4,1,4,128]{3,2,1,0:T(4,128)S(1)}, f32[4,1,4,128]{3,2,1,0:T(4,128)S(1)}, u32[]{:S(2)}, u32[]{:S(2)}) collective-permute-start(f32[4,1,4,128]{3,2,1,0:T(4,128)S(1)} %get-tuple-element.566), channel_id=1, source_target_pairs={{0,2},{2,4},{4,6},{1,3},{3,5},{5,7},{8,10},{10,12},{12,14},{9,11},... | collective-permute-start | bytes 24584 | tf_op jit(solution)/shard_map/ppermute | solution.py:45
  168.5 4.4 %collective-permute-start.13 = (f32[4,1,4,128]{3,2,1,0:T(4,128)S(1)}, f32[4,1,4,128]{3,2,1,0:T(4,128)S(1)}, u32[]{:S(2)}, u32[]{:S(2)}) collective-permute-start(f32[4,1,4,128]{3,2,1,0:T(4,128)S(1)} %get-tuple-element.567), channel_id=1, source_target_pairs={{2,0},{4,2},{6,4},{3,1},{5,3},{7,5},{10,8},{12,10},{14,12},{11,9},... | collective-permute-start | bytes 24584 | tf_op jit(solution)/shard_map/ppermute | solution.py:47
  172.9 4.6 %collective-permute-start.14 = (f32[4,6,1,128]{3,2,1,0:T(1,128)S(1)}, f32[4,6,1,128]{3,2,1,0:T(1,128)S(1)}, u32[]{:S(2)}, u32[]{:S(2)}) collective-permute-start(f32[4,6,1,128]{3,2,1,0:T(1,128)S(1)} %get-tuple-element.557), channel_id=1, source_target_pairs={{0,1},{2,3},{4,5},{6,7},{8,9},{10,11},{12,13},{14,15},{16,17},{18,... | collective-permute-start | bytes 36872 | tf_op jit(solution)/shard_map/ppermute | solution.py:45
  176.2 4.4 %collective-permute-start.15 = (f32[4,6,1,128]{3,2,1,0:T(1,128)S(1)}, f32[4,6,1,128]{3,2,1,0:T(1,128)S(1)}, u32[]{:S(2)}, u32[]{:S(2)}) collective-permute-start(f32[4,6,1,128]{3,2,1,0:T(1,128)S(1)} %get-tuple-element.558), channel_id=1, source_target_pairs={{1,0},{3,2},{5,4},{7,6},{9,8},{11,10},{13,12},{15,14},{17,16},{19,... | collective-permute-start | bytes 36872 | tf_op jit(solution)/shard_map/ppermute | solution.py:47
  224.7 8.1 %collective-permute-start.16 = (f32[4,3,128]{2,1,0:T(4,128)S(1)}, f32[4,3,128]{2,1,0:T(4,128)S(1)}, u32[]{:S(2)}, u32[]{:S(2)}) collective-permute-start(f32[4,3,128]{2,1,0:T(4,128)S(1)} %get-tuple-element.563), channel_id=1, source_target_pairs={{0,8},{8,16},{16,24},{24,0},{1,9},{9,17},{17,25},{25,1},{2,10},{10... | collective-permute-start | bytes 18440 | tf_op jit(solution)/shard_map/ppermute | solution.py:57
  227.0 6.4 %collective-permute-start.17 = (f32[4,3,128]{2,1,0:T(4,128)S(1)}, f32[4,3,128]{2,1,0:T(4,128)S(1)}, u32[]{:S(2)}, u32[]{:S(2)}) collective-permute-start(f32[4,3,128]{2,1,0:T(4,128)S(1)} %get-tuple-element.565), channel_id=1, source_target_pairs={{0,16},{8,24},{16,0},{24,8},{1,17},{9,25},{17,1},{25,9},{2,18},{10... | collective-permute-start | bytes 18440 | tf_op jit(solution)/shard_map/ppermute | solution.py:57
  232.1 3.1 %collective-permute-start.18 = (f32[4,3,128]{2,1,0:T(4,128)S(1)}, f32[4,3,128]{2,1,0:T(4,128)S(1)}, u32[]{:S(2)}, u32[]{:S(2)}) collective-permute-start(f32[4,3,128]{2,1,0:T(4,128)S(1)} %get-tuple-element.564), channel_id=1, source_target_pairs={{0,24},{8,0},{16,8},{24,16},{1,25},{9,1},{17,9},{25,17},{2,26},{10... | collective-permute-start | bytes 18440 | tf_op jit(solution)/shard_map/ppermute | solution.py:57
